TPU v7x, 32 devices: a whole 2x2x4 slice. The times are simulated.
32 devices in a mesh: blk: 16 (over z, y, core), rel: 2 (over x).
Axes of the slice: x: 2, y: 2, z: 4, core: 2. Of those that a mesh axis runs over, the one named last changes fastest.
Arguments:
- words: bfloat16 [4096, 800], P('blk'), may hold values from -1.5 to 1.5
- contexts: bfloat16 [4096, 800], P('blk'), may hold values from -1.5 to 1.5
- relations: bfloat16 [1024, 800], P(('blk', 'rel')), may hold values from -6 to 6
- word_index: int32 [8192], P(('blk', 'rel')), may hold values from 0 to 255
- context_index: int32 [8192], P(('blk', 'rel')), may hold values from 0 to 255
- rel_slot: int32 [8192], P(('blk', 'rel')), may hold values from 0 to 63, as said below
- neg_index: int32 [32, 1024], P(('blk', 'rel')), may hold values from 0 to 255
- requests: int32 [16, 2, 16, 2, 2], P('blk', 'rel'), may hold values from 0 to 31, as said below
- counts: int32 [16, 2, 16, 2], P('blk', 'rel'), may hold values from 0 to 2, as said below
Outputs:
- word_grad: bfloat16 [4096, 800], P('blk')
- context_grad: bfloat16 [4096, 800], P('blk')
- relation_grad: float32 [1024, 800], P(('blk', 'rel'))
Inputs may be any that keep to these rules, and one draw needn't show every extreme that they name: counts[b, r, b2, r2] is how many entries of the list of device (b, r) to owner (b2, r2) are live; each device's list to itself is full, and so are all lists to one owner. requests[b, r, b2, r2, k] is a row among the 32 relation rows of owner (b2, r2); the live entries of one list are distinct and come first, the others are 0. rel_slot of a triple of device (b, r) is a live slot s = (b2 * 2 + r2) * 2 + k of that device, with k < counts[b, r, b2, r2].
All inputs are finite; a program needn't handle non-finite values.
Results may differ from a plain program's by a relative error of at most 0.013.
Values may be sent and summed in bfloat16 or wider, within the bound.
No kernel may reach another device: no remote copies, remote signals or barrier semaphores. Data moves between devices by JAX's collectives and lax.ppermute only.
A program may use at most 64 MiB of HBM per device.

v0:
```python
import jax
import jax.numpy as jnp
from jax import lax
from jax.sharding import PartitionSpec as P


def passed_along(shard, axis, by):
    length = lax.axis_size(axis)
    return lax.ppermute(shard, axis, [(i, (i + by) % length) for i in range(length)])


def complex_product(left_vec, right_vec, half_width):
    left_re, left_im = (left_vec[:, :half_width], left_vec[:, half_width:])
    right_re, right_im = (right_vec[:, :half_width], right_vec[:, half_width:])
    return jnp.concatenate(
        [left_re * right_re - left_im * right_im, left_re * right_im + left_im * right_re], axis=1
    )


def conj_product(grad_vec, other_vec, half_width):
    grad_re, grad_im = (grad_vec[:, :half_width], grad_vec[:, half_width:])
    other_re, other_im = (other_vec[:, :half_width], other_vec[:, half_width:])
    return jnp.concatenate(
        [grad_re * other_re + grad_im * other_im, grad_im * other_re - grad_re * other_im], axis=1
    )


def one_hot_rows(index_ids, row_total):
    return (jnp.arange(row_total)[:, None] == index_ids[None, :]).astype(jnp.bfloat16)


def spread_rows(selector, terms):
    upper = terms.astype(jnp.bfloat16)
    lower = (terms - upper.astype(jnp.float32)).astype(jnp.bfloat16)
    return jnp.dot(selector, upper, preferred_element_type=jnp.float32) + jnp.dot(
        selector, lower, preferred_element_type=jnp.float32
    )


def shards(
    words, contexts, relations, word_index, context_index, rel_slot, neg_index, requests, counts
):
    row_width = words.shape[1]
    half_width = row_width // 2
    part_count = lax.axis_size("blk")
    split_count = lax.axis_size("rel")
    slot_count = requests.shape[-1]
    owned_rows = relations.shape[0]
    block_count = neg_index.shape[0]
    block_size = word_index.shape[0] // block_count
    part_rows = contexts.shape[0]
    neg_scale = float(neg_index.shape[1]) ** (-0.5)
    held_rows = passed_along(contexts, "blk", 1)
    wanted = requests[0, 0]
    incoming = lax.all_to_all(
        lax.all_to_all(wanted, "blk", split_axis=0, concat_axis=0, tiled=True),
        "rel",
        split_axis=1,
        concat_axis=1,
        tiled=True,
    )
    picked = relations[incoming.reshape(-1)].reshape(part_count, split_count, slot_count, row_width)
    fetched = lax.all_to_all(
        lax.all_to_all(picked, "blk", split_axis=0, concat_axis=0, tiled=True),
        "rel",
        split_axis=1,
        concat_axis=1,
        tiled=True,
    )
    slot_table = fetched.reshape(-1, row_width)
    slot_total = slot_table.shape[0]
    live_mask = (
        (jnp.arange(slot_count)[None, None, :] < counts[0, 0][:, :, None])
        .reshape(-1)
        .astype(jnp.float32)
    )
    word_used = words[word_index]
    ctx_used = held_rows[context_index]
    rel_used = slot_table[rel_slot]
    query = complex_product(
        word_used.astype(jnp.float32), rel_used.astype(jnp.float32), half_width
    ).astype(jnp.bfloat16)
    positive = jnp.einsum("td,td->t", query, ctx_used, preferred_element_type=jnp.float32)
    pos_grad = -jax.nn.sigmoid(-positive)
    ctx_start = spread_rows(
        one_hot_rows(context_index, part_rows), pos_grad[:, None] * query.astype(jnp.float32)
    )

    def block_step(ctx_total, inputs_one):
        query_block, ctx_block, neg_block, pos_block = inputs_one
        selector = one_hot_rows(neg_block, part_rows)
        neg_rows = lax.dot_general(
            selector, held_rows, (((0,), (0,)), ((), ())), preferred_element_type=jnp.float32
        ).astype(jnp.bfloat16)
        scores = lax.dot_general(
            query_block, neg_rows, (((1,), (1,)), ((), ())), preferred_element_type=jnp.float32
        )
        neg_grad = (jax.nn.sigmoid(scores) * neg_scale).astype(jnp.bfloat16)
        query_grad = pos_block[:, None] * ctx_block.astype(jnp.float32) + jnp.dot(
            neg_grad, neg_rows, preferred_element_type=jnp.float32
        )
        back_rows = lax.dot_general(
            neg_grad, query_block, (((0,), (0,)), ((), ())), preferred_element_type=jnp.float32
        )
        return (ctx_total + spread_rows(selector, back_rows), query_grad)

    ctx_part, query_grads = lax.scan(
        block_step,
        ctx_start,
        (
            query.reshape(block_count, block_size, row_width),
            ctx_used.reshape(block_count, block_size, row_width),
            neg_index,
            pos_grad.reshape(block_count, block_size),
        ),
    )
    query_grads = query_grads.reshape(-1, row_width)
    word_part = spread_rows(
        one_hot_rows(word_index, words.shape[0]),
        conj_product(query_grads, rel_used.astype(jnp.float32), half_width),
    )
    slot_grad = spread_rows(
        one_hot_rows(rel_slot, slot_total),
        conj_product(query_grads, word_used.astype(jnp.float32), half_width),
    )
    slot_grad = slot_grad + 0.02 * live_mask[:, None] * slot_table.astype(jnp.float32)
    word_sum, ctx_sum = (
        lax.psum(word_part.astype(jnp.bfloat16), "rel").astype(jnp.float32),
        lax.psum(ctx_part.astype(jnp.bfloat16), "rel").astype(jnp.float32),
    )
    outgoing = slot_grad.reshape(part_count, split_count, slot_count, row_width)
    returned = lax.all_to_all(
        lax.all_to_all(
            outgoing.astype(jnp.bfloat16), "blk", split_axis=0, concat_axis=0, tiled=True
        ),
        "rel",
        split_axis=1,
        concat_axis=1,
        tiled=True,
    ).astype(outgoing.dtype)
    owner_map = (incoming.reshape(-1)[None, :] == jnp.arange(owned_rows)[:, None]).astype(
        jnp.float32
    )
    relation_grad = jnp.dot(
        owner_map,
        returned.reshape(-1, row_width),
        precision=lax.Precision.HIGHEST,
        preferred_element_type=jnp.float32,
    )
    return (word_sum.astype(jnp.bfloat16), ctx_sum.astype(jnp.bfloat16), relation_grad)


def solution(mesh):
    return jax.shard_map(
        shards,
        mesh=mesh,
        in_specs=(
            P("blk", None),
            P("blk", None),
            P(("blk", "rel"), None),
            P(("blk", "rel")),
            P(("blk", "rel")),
            P(("blk", "rel")),
            P(("blk", "rel"), None),
            P("blk", "rel", None, None, None),
            P("blk", "rel", None, None),
        ),
        out_specs=(P("blk", None), P("blk", None), P(("blk", "rel"), None)),
        check_vma=False,
    )
```

profile of v0, /device:TPU:0, one launch (start us, length us, event | category | flops | bytes accessed | tf_op | source)
XLA Modules:
  0.0 111.6 jit_solution(12965899353701402154)
XLA Ops:
  7.2 1.4 %copy.51 = s32[16,2,2]{2,1,0:T(2,128)} copy(s32[16,2,2]{0,2,1:T(2,128)} %bitcast.14) | data formatting | bytes 512 | tf_op jit(solution)/shard_map/squeeze | solution.py:54
  8.6 7.4 %all-to-all-start = ((s32[16,2,2]{2,1,0:T(2,128)}), s32[16,2,2]{2,1,0:T(2,128)S(1)}, u32[]{:S(2)}, u32[]{:S(2)}) async-start(s32[16,2,2]{2,1,0:T(2,128)} %copy.51), calls=%async_computation | async-start | bytes 32768 | tf_op jit(solution)/shard_map/all_to_all | solution.py:56
  16.0 2.0 %copy.57 = bf16[256,800]{1,0:T(8,128)(2,1)} copy(bf16[256,800]{0,1:T(8,128)(2,1)} %param.10) | data formatting | bytes 819200 | tf_op args[1]
  20.6 1.9 %all-to-all-done = s32[16,2,2]{2,1,0:T(2,128)S(1)} async-done(((s32[16,2,2]{2,1,0:T(2,128)}), s32[16,2,2]{2,1,0:T(2,128)S(1)}, u32[]{:S(2)}, u32[]{:S(2)}) %all-to-all-start) | async-done | bytes 288 | tf_op jit(solution)/shard_map/all_to_all | solution.py:56
  23.2 3.2 %all-to-all-start.1 = ((s32[16,2,2]{0,2,1:T(2,128)}), s32[16,2,2]{0,2,1:T(2,128)S(1)}, u32[]{:S(2)}, u32[]{:S(2)}) async-start(s32[16,2,2]{0,2,1:T(2,128)} %copy.52), calls=%async_computation.1 | async-start | bytes 4096 | tf_op jit(solution)/shard_map/all_to_all | solution.py:55
  26.4 3.7 %all-to-all-done.1 = s32[16,2,2]{0,2,1:T(2,128)S(1)} async-done(((s32[16,2,2]{0,2,1:T(2,128)}), s32[16,2,2]{0,2,1:T(2,128)S(1)}, u32[]{:S(2)}, u32[]{:S(2)}) %all-to-all-start.1) | async-done | bytes 288 | tf_op jit(solution)/shard_map/all_to_all | solution.py:55
  31.8 3.9 %all-to-all-start.2 = ((bf16[16,2,2,800]{3,2,1,0:T(2,128)(2,1)}), bf16[16,2,2,800]{3,2,1,0:T(2,128)(2,1)S(1)}, u32[]{:S(2)}, u32[]{:S(2)}) async-start(bf16[16,2,2,800]{3,2,1,0:T(2,128)(2,1)} %reshape.86), calls=%async_computation.2 | async-start | bytes 229376 | tf_op jit(solution)/shard_map/all_to_all | solution.py:64
  35.7 7.7 %all-to-all-done.2 = bf16[16,2,2,800]{3,2,1,0:T(2,128)(2,1)S(1)} async-done(((bf16[16,2,2,800]{3,2,1,0:T(2,128)(2,1)}), bf16[16,2,2,800]{3,2,1,0:T(2,128)(2,1)S(1)}, u32[]{:S(2)}, u32[]{:S(2)}) %all-to-all-start.2) | async-done | bytes 102432 | tf_op jit(solution)/shard_map/all_to_all | solution.py:64
  44.1 3.4 %all-to-all-start.3 = ((bf16[16,2,2,800]{3,2,0,1:T(2,128)(2,1)}), bf16[16,2,2,800]{3,2,0,1:T(2,128)(2,1)S(1)}, u32[]{:S(2)}, u32[]{:S(2)}) async-start(bf16[16,2,2,800]{3,2,0,1:T(2,128)(2,1)} %copy.54), calls=%async_computation.3 | async-start | bytes 229376 | tf_op jit(solution)/shard_map/all_to_all | solution.py:63
  47.8 1.2 %gather_fusion = bf16[256,800]{1,0:T(8,128)(2,1)S(1)} fusion(bf16[256,800]{1,0:T(8,128)(2,1)S(1)} %copy.49, s32[1024]{0:T(1024)S(1)} %pad_clamp_fusion.3), kind=kCustom, calls=%fused_computation | custom fusion | bytes 820224 | tf_op jit(solution)/shard_map/gather | solution.py:77
  49.4 2.5 %all-to-all-done.3 = bf16[16,2,2,800]{3,2,0,1:T(2,128)(2,1)S(1)} async-done(((bf16[16,2,2,800]{3,2,0,1:T(2,128)(2,1)}), bf16[16,2,2,800]{3,2,0,1:T(2,128)(2,1)S(1)}, u32[]{:S(2)}, u32[]{:S(2)}) %all-to-all-start.3) | async-done | bytes 102432 | tf_op jit(solution)/shard_map/all_to_all | solution.py:63
  52.0 1.2 %gather_fusion.2 = bf16[256,800]{1,0:T(8,128)(2,1)S(1)} fusion(bf16[64,800]{1,0:T(8,128)(2,1)S(1)} %reshape.87, s32[1024]{0:T(1024)S(1)} %pad_clamp_fusion.1), kind=kCustom, calls=%fused_computation.2 | custom fusion | bytes 820224 | tf_op jit(solution)/shard_map/gather | solution.py:79
  53.7 1.2 %copy.66 = f32[256,800]{1,0:T(8,128)} copy(f32[256,800]{0,1:T(8,128)S(1)} %fusion.41) | data formatting | bytes 1638400
  56.5 1.5 %fusion.42 = f32[256,800]{0,1:T(8,128)} fusion(bf16[256,1024]{1,0:T(8,128)(2,1)S(1)} %fusion.6, bf16[1024,800]{0,1:T(8,128)(2,1)S(1)} %convolution_convert_fusion), kind=kOutput, calls=%fused_computation.81 | convolution fusion | flops 419430400 | bytes 2981888 | tf_op jit(solution)/shard_map/while/body/eval_jaxpr/dot_general | solution.py:99
  58.0 2.3 %fusion.40 = f32[1024,800]{0,1:T(8,128)} fusion(bf16[256,1024]{1,0:T(8,128)(2,1)S(1)} %fusion.6, bf16[256,400]{0,1:T(8,128)(2,1)S(1)} %get-tuple-element.34, bf16[256,400]{0,1:T(8,128)(2,1)S(1)} %get-tuple-element.33), kind=kOutput, calls=%fused_computation.79 | convolution fusion | flops 420249600 | bytes 4210688 | tf_op jit(solution)/shard_map/while/body/eval_jaxpr/dot_general | solution.py:102
  60.3 1.2 %gather_fusion.3 = bf16[256,800]{1,0:T(8,128)(2,1)S(1)} fusion(bf16[256,800]{1,0:T(8,128)(2,1)S(1)} %collective-permute-done, s32[1024]{0:T(1024)S(1)} %pad_clamp_fusion), kind=kCustom, calls=%fused_computation.3 | custom fusion | bytes 820224 | tf_op jit(solution)/shard_map/gather | solution.py:78
  61.7 1.4 %multiply_reduce_fusion = f32[256]{0:T(256)S(1)} fusion(f32[256,800]{1,0:T(8,128)} %copy.66, bf16[256,800]{1,0:T(8,128)(2,1)S(1)} %gather_fusion.3), kind=kLoop, calls=%fused_computation.23 | loop fusion | flops 614144 | bytes 1229824 | tf_op jit(solution)/shard_map/td,td->t/dot_general | solution.py:83
  67.7 1.4 %fusion.8 = bf16[256,800]{0,1:T(8,128)(2,1)} fusion(f32[256,800]{0,1:T(8,128)S(1)} %convolution_add_fusion.1, f32[256,800]{0,1:T(8,128)S(1)} %fusion, f32[1024,800]{0,1:T(8,128)S(1)} %copy-done.1, s32[1024]{0:T(1024)S(1)} %bitcast.13), kind=kOutput, calls=%fused_computation.18 | convolution fusion | flops 421126144 | bytes 5328896 | tf_op jit(solution)/shard_map/while/body/eval_jaxpr/dot_general | solution.py:35
  69.8 10.3 %all_to_all.30 = bf16[16,2,2,800]{3,2,1,0:T(2,128)(2,1)S(1)} all-to-all(bf16[16,2,2,800]{3,2,1,0:T(2,128)(2,1)S(1)} %convert_element_type.113), channel_id=1, replica_groups=mesh['blk'=16,'rel'=2] {'blk'}, dimensions={0} | all-to-all | bytes 204800 | tf_op jit(solution)/shard_map/all_to_all | solution.py:133
  80.8 3.4 %all-to-all-start.5 = ((bf16[16,2,2,800]{3,2,0,1:T(2,128)(2,1)}), bf16[16,2,2,800]{3,2,0,1:T(2,128)(2,1)S(1)}, u32[]{:S(2)}, u32[]{:S(2)}) async-start(bf16[16,2,2,800]{3,2,0,1:T(2,128)(2,1)} %copy.61), calls=%async_computation.5 | async-start | bytes 229376 | tf_op jit(solution)/shard_map/all_to_all | solution.py:132
  84.3 4.3 %all-to-all-done.5 = bf16[16,2,2,800]{3,2,0,1:T(2,128)(2,1)S(1)} async-done(((bf16[16,2,2,800]{3,2,0,1:T(2,128)(2,1)}), bf16[16,2,2,800]{3,2,0,1:T(2,128)(2,1)S(1)}, u32[]{:S(2)}, u32[]{:S(2)}) %all-to-all-start.5) | async-done | bytes 102432 | tf_op jit(solution)/shard_map/all_to_all | solution.py:132
  89.5 11.7 %all-reduce.3.cloned.1.call-done = (bf16[256,800]{0,1:T(8,128)(2,1)}, bf16[256,800]{0,1:T(8,128)(2,1)}) async-done(((bf16[256,800]{0,1:T(8,128)(2,1)}, bf16[256,800]{0,1:T(8,128)(2,1)}), (bf16[256,800]{0,1:T(8,128)(2,1)}, bf16[256,800]{0,1:T(8,128)(2,1)})) %all-reduce.3.cloned.1.call-update) | async-done | bytes 819216 | tf_op jit(solution)/shard_map/psum | solution.py:128
  101.2 1.8 %copy.69 = bf16[256,800]{0,1:T(8,128)(2,1)} copy(bf16[256,800]{0,1:T(8,128)(2,1)} %get-tuple-element.37) | data formatting | bytes 819200
  103.0 1.8 %copy.70 = bf16[256,800]{0,1:T(8,128)(2,1)} copy(bf16[256,800]{0,1:T(8,128)(2,1)} %get-tuple-element.38) | data formatting | bytes 819200
  (67 shorter events, 15.6 us)
Async XLA Ops:
  7.2 23.2 %copy-start = (bf16[32,800]{1,0:T(8,128)(2,1)S(1)}, bf16[32,800]{1,0:T(8,128)(2,1)}, u32[]{:S(2)}) copy-start(bf16[32,800]{1,0:T(8,128)(2,1)} %param.11) | copy-start | bytes 153604
  7.2 28.5 %copy-start.7 = (s32[256]{0:T(256)S(1)}, s32[256]{0:T(256)}, u32[]{:S(2)}) copy-start(s32[256]{0:T(256)} %param.13) | copy-start | bytes 3076
  7.2 40.3 %copy-start.4 = (bf16[256,800]{0,1:T(8,128)(2,1)S(1)}, bf16[256,800]{0,1:T(8,128)(2,1)}, u32[]{:S(2)}) copy-start(bf16[256,800]{0,1:T(8,128)(2,1)} %param.9) | copy-start | bytes 1228804
  8.6 13.9 %all-to-all-start = ((s32[16,2,2]{2,1,0:T(2,128)}), s32[16,2,2]{2,1,0:T(2,128)S(1)}, u32[]{:S(2)}, u32[]{:S(2)}) async-start(s32[16,2,2]{2,1,0:T(2,128)} %copy.51), calls=%async_computation | async-start | bytes 32768 | tf_op jit(solution)/shard_map/all_to_all | solution.py:56
  18.0 36.9 %collective-permute-start = (bf16[256,800]{1,0:T(8,128)(2,1)}, bf16[256,800]{1,0:T(8,128)(2,1)S(1)}, u32[]{:S(2)}, u32[]{:S(2)}) collective-permute-start(bf16[256,800]{1,0:T(8,128)(2,1)} %copy.57), channel_id=1, source_target_pairs={{0,2},{2,4},{4,6},{6,8},{8,10},{10,12},{12,14},{14,16},{16,18},{18... | collective-permute-start | bytes 1228808 | tf_op jit(solution)/shard_map/ppermute | solution.py:9
  23.2 7.0 %all-to-all-start.1 = ((s32[16,2,2]{0,2,1:T(2,128)}), s32[16,2,2]{0,2,1:T(2,128)S(1)}, u32[]{:S(2)}, u32[]{:S(2)}) async-start(s32[16,2,2]{0,2,1:T(2,128)} %copy.52), calls=%async_computation.1 | async-start | bytes 4096 | tf_op jit(solution)/shard_map/all_to_all | solution.py:55
  31.8 11.6 %all-to-all-start.2 = ((bf16[16,2,2,800]{3,2,1,0:T(2,128)(2,1)}), bf16[16,2,2,800]{3,2,1,0:T(2,128)(2,1)S(1)}, u32[]{:S(2)}, u32[]{:S(2)}) async-start(bf16[16,2,2,800]{3,2,1,0:T(2,128)(2,1)} %reshape.86), calls=%async_computation.2 | async-start | bytes 229376 | tf_op jit(solution)/shard_map/all_to_all | solution.py:64
  44.1 7.7 %all-to-all-start.3 = ((bf16[16,2,2,800]{3,2,0,1:T(2,128)(2,1)}), bf16[16,2,2,800]{3,2,0,1:T(2,128)(2,1)S(1)}, u32[]{:S(2)}, u32[]{:S(2)}) async-start(bf16[16,2,2,800]{3,2,0,1:T(2,128)(2,1)} %copy.54), calls=%async_computation.3 | async-start | bytes 229376 | tf_op jit(solution)/shard_map/all_to_all | solution.py:63
  47.5 53.8 %all-reduce.3.cloned.1.call-start = ((), (), s32[]{:S(2)}) async-start(), calls=%async_computation.6 | async-start | bytes 1638400 | tf_op jit(solution)/shard_map/psum | solution.py:128
  53.6 1.3 %copy-start.5 = (s32[1,1024]{1,0:T(1,128)S(1)}, s32[1,1024]{1,0:T(1,128)}, u32[]{:S(2)}) copy-start(s32[1,1024]{1,0:T(1,128)} %param.15) | copy-start | bytes 12292
  61.7 1.8 %copy-start.3 = (f32[256,800]{0,1:T(8,128)S(1)}, f32[256,800]{0,1:T(8,128)}, u32[]{:S(2)}) copy-start(f32[256,800]{0,1:T(8,128)} %fusion.42) | copy-start | bytes 2457604
  63.6 2.1 %copy-start.1 = (f32[1024,800]{0,1:T(8,128)S(1)}, f32[1024,800]{0,1:T(8,128)}, u32[]{:S(2)}) copy-start(f32[1024,800]{0,1:T(8,128)} %fusion.40) | copy-start | bytes 9830404
  65.7 0.7 copy-start.6
  67.7 1.5 %copy-start.2 = (f32[256,400]{0,1:T(8,128)S(1)}, f32[256,400]{0,1:T(8,128)}, u32[]{:S(2)}) copy-start(f32[256,400]{0,1:T(8,128)} %get-tuple-element.22) | copy-start | bytes 1228804
  67.7 1.5 %copy-start.8 = (s32[256]{0:T(256)S(1)}, s32[256]{0:T(256)}, u32[]{:S(2)}) copy-start(s32[256]{0:T(256)} %param.14) | copy-start | bytes 3076
  80.8 7.7 %all-to-all-start.5 = ((bf16[16,2,2,800]{3,2,0,1:T(2,128)(2,1)}), bf16[16,2,2,800]{3,2,0,1:T(2,128)(2,1)S(1)}, u32[]{:S(2)}, u32[]{:S(2)}) async-start(bf16[16,2,2,800]{3,2,0,1:T(2,128)(2,1)} %copy.61), calls=%async_computation.5 | async-start | bytes 229376 | tf_op jit(solution)/shard_map/all_to_all | solution.py:132
Sparse Core Ops, SparseCore 0:
  69.3 31.8 all-reduce.2
where the time goes:
time: 112 us
  waiting for transfers between devices  31.8 us (28%)
  starting transfers between devices  21.6 us (19%)
  local copies, waits for them, and re-layouts  18.5 us (17%)
  between operations  14.4 us (13%)
  matrix products  10.8 us (10%)
  blocking collectives  10.3 us (9%)
  other arithmetic  4.32 us (4%)
    psum x1, waiting for transfers between devices, shards(): lax.psum(word_part.astype(jnp.bfloat16), 'rel').astype(jnp.float32)  11.7 us
    all_to_all x1, blocking collectives, shards(): lax.all_to_all(outgoing.astype(jnp.bfloat16), 'blk', split_axis=0, concat...  10.3 us
    unnamed x23, local copies, waits for them, and re-layouts  7.83 us
    all_to_all x1, waiting for transfers between devices, shards(): lax.all_to_all(picked, 'blk', split_axis=0, concat_axis=0, tiled=True)  7.65 us
    all_to_all x1, starting transfers between devices, shards(): lax.all_to_all(wanted, 'blk', split_axis=0, concat_axis=0, tiled=True)  7.39 us
    all_to_all x1, waiting for transfers between devices, shards(): lax.all_to_all(lax.all_to_all(outgoing.astype(jnp.bfloat16), 'blk', split...  4.26 us
    all_to_all x1, starting transfers between devices, shards(): lax.all_to_all(picked, 'blk', split_axis=0, concat_axis=0, tiled=True)  3.87 us
    all_to_all x1, waiting for transfers between devices, shards(): lax.all_to_all(lax.all_to_all(wanted, 'blk', split_axis=0, concat_axis=0,...  3.75 us
  transfers between devices with their start and end apart: 7, of which 6 were waited for; matrix products, arithmetic and copies ran while one was open for 13% of the time, Pallas kernels for 0%

commit v1 on v0

--- a/solution.py
+++ b/solution.py
@@ -125,7 +125,7 @@
     )
     slot_grad = slot_grad + 0.02 * live_mask[:, None] * slot_table.astype(jnp.float32)
     word_sum, ctx_sum = (
-        lax.psum(word_part.astype(jnp.bfloat16), "rel").astype(jnp.float32),
+        jnp.sum(lax.all_gather(word_part.astype(jnp.bfloat16), "rel"), axis=0).astype(jnp.float32),
         lax.psum(ctx_part.astype(jnp.bfloat16), "rel").astype(jnp.float32),
     )
     outgoing = slot_grad.reshape(part_count, split_count, slot_count, row_width)

time: 112 us -> 117 us (1.045)
  waiting for transfers between devices: 31.8 us -> 21 us
  other arithmetic: 4.32 us -> 8.27 us
  starting transfers between devices: 21.6 us -> 25.5 us
  matrix products: 10.8 us -> 14.1 us
  blocking collectives: 10.3 us -> 13.4 us
    all_gather x0 -> x1, blocking collectives: none -> 13.4 us  [shards(): lax.all_gather(word_part.astype(jnp.bfloat16), 'rel')]
    all_to_all x1 -> x0, blocking collectives: 10.3 us -> none  [shards(): lax.all_to_all(outgoing.astype(jnp.bfloat16), 'blk', split_axis=0, concat...]
    psum x1, waiting for transfers between devices: 11.7 us -> 2.63 us  [shards(): lax.psum(ctx_part.astype(jnp.bfloat16), 'rel').astype(jnp.float32)]
    all_to_all x1, waiting for transfers between devices: 4.26 us -> 0.01 us  [shards(): lax.all_to_all(lax.all_to_all(outgoing.astype(jnp.bfloat16), 'blk', split...]
    all_to_all x0 -> x1, starting transfers between devices: none -> 4.15 us  [shards(): lax.all_to_all(outgoing.astype(jnp.bfloat16), 'blk', split_axis=0, concat...]
    reduce_sum x0 -> x1, other arithmetic: none -> 2.93 us  [shards(): jnp.sum(lax.all_gather(word_part.astype(jnp.bfloat16), 'rel'), axis=0)]
    unnamed x23 -> x28, local copies, waits for them, and re-layouts: 7.83 us -> 5.7 us
    dot_general x4, matrix products: 2.33 us -> 4.39 us  [spread_rows(): jnp.dot(selector, upper, preferred_element_type=jnp.float32)]
  transfers between devices with their start and end apart: 7 -> 8, of which waited for: 6 -> 6; matrix products, arithmetic and copies ran while one was open for 13% -> 21% of each run, Pallas kernels for 0% -> 0%
where the time goes in v1:
time: 117 us; the launch traced here: 116 us
  starting transfers between devices  25.5 us (22%)
  waiting for transfers between devices  21 us (18%)
  local copies, waits for them, and re-layouts  19.1 us (16%)
  between operations  14.4 us (12%)
  matrix products  14.1 us (12%)
  blocking collectives  13.4 us (11%)
  other arithmetic  8.27 us (7%)
    all_gather x1, blocking collectives, shards(): lax.all_gather(word_part.astype(jnp.bfloat16), 'rel')  13.4 us
    all_to_all x1, waiting for transfers between devices, shards(): lax.all_to_all(picked, 'blk', split_axis=0, concat_axis=0, tiled=True)  7.61 us
    all_to_all x1, starting transfers between devices, shards(): lax.all_to_all(wanted, 'blk', split_axis=0, concat_axis=0, tiled=True)  7.39 us
    unnamed x28, local copies, waits for them, and re-layouts  5.7 us
    dot_general x4, matrix products, spread_rows(): jnp.dot(selector, upper, preferred_element_type=jnp.float32)  4.39 us
    all_to_all x1, starting transfers between devices, shards(): lax.all_to_all(outgoing.astype(jnp.bfloat16), 'blk', split_axis=0, concat...  4.15 us
    all_to_all x1, waiting for transfers between devices, shards(): lax.all_to_all(lax.all_to_all(wanted, 'blk', split_axis=0, concat_axis=0,...  3.75 us
    dot_general x4, matrix products, spread_rows(): jnp.dot(selector, lower, preferred_element_type=jnp.float32)  3.57 us
  transfers between devices with their start and end apart: 8, of which 6 were waited for; matrix products, arithmetic and copies ran while one was open for 21% of the time, Pallas kernels for 0%

profile of v1, /device:TPU:0, one launch (start us, length us, event | category | flops | bytes accessed | tf_op | source)
XLA Modules:
  0.0 115.7 jit_solution(17299743178935162796)
XLA Ops:
  7.2 1.4 %copy.51 = s32[16,2,2]{2,1,0:T(2,128)} copy(s32[16,2,2]{0,2,1:T(2,128)} %bitcast.16) | data formatting | bytes 512 | tf_op jit(solution)/shard_map/squeeze | solution.py:54
  8.6 7.4 %all-to-all-start = ((s32[16,2,2]{2,1,0:T(2,128)}), s32[16,2,2]{2,1,0:T(2,128)S(1)}, u32[]{:S(2)}, u32[]{:S(2)}) async-start(s32[16,2,2]{2,1,0:T(2,128)} %copy.51), calls=%async_computation | async-start | bytes 32768 | tf_op jit(solution)/shard_map/all_to_all | solution.py:56
  19.9 2.6 %all-to-all-done = s32[16,2,2]{2,1,0:T(2,128)S(1)} async-done(((s32[16,2,2]{2,1,0:T(2,128)}), s32[16,2,2]{2,1,0:T(2,128)S(1)}, u32[]{:S(2)}, u32[]{:S(2)}) %all-to-all-start) | async-done | bytes 288 | tf_op jit(solution)/shard_map/all_to_all | solution.py:56
  23.2 3.2 %all-to-all-start.1 = ((s32[16,2,2]{0,2,1:T(2,128)}), s32[16,2,2]{0,2,1:T(2,128)S(1)}, u32[]{:S(2)}, u32[]{:S(2)}) async-start(s32[16,2,2]{0,2,1:T(2,128)} %copy.52), calls=%async_computation.1 | async-start | bytes 4096 | tf_op jit(solution)/shard_map/all_to_all | solution.py:55
  26.4 3.7 %all-to-all-done.1 = s32[16,2,2]{0,2,1:T(2,128)S(1)} async-done(((s32[16,2,2]{0,2,1:T(2,128)}), s32[16,2,2]{0,2,1:T(2,128)S(1)}, u32[]{:S(2)}, u32[]{:S(2)}) %all-to-all-start.1) | async-done | bytes 288 | tf_op jit(solution)/shard_map/all_to_all | solution.py:55
  31.8 3.5 %all-to-all-start.2 = ((bf16[16,2,2,800]{3,2,1,0:T(2,128)(2,1)}), bf16[16,2,2,800]{3,2,1,0:T(2,128)(2,1)S(1)}, u32[]{:S(2)}, u32[]{:S(2)}) async-start(bf16[16,2,2,800]{3,2,1,0:T(2,128)(2,1)} %reshape.86), calls=%async_computation.2 | async-start | bytes 229376 | tf_op jit(solution)/shard_map/all_to_all | solution.py:64
  35.4 7.6 %all-to-all-done.2 = bf16[16,2,2,800]{3,2,1,0:T(2,128)(2,1)S(1)} async-done(((bf16[16,2,2,800]{3,2,1,0:T(2,128)(2,1)}), bf16[16,2,2,800]{3,2,1,0:T(2,128)(2,1)S(1)}, u32[]{:S(2)}, u32[]{:S(2)}) %all-to-all-start.2) | async-done | bytes 102432 | tf_op jit(solution)/shard_map/all_to_all | solution.py:64
  43.7 3.4 %all-to-all-start.3 = ((bf16[16,2,2,800]{3,2,0,1:T(2,128)(2,1)}), bf16[16,2,2,800]{3,2,0,1:T(2,128)(2,1)S(1)}, u32[]{:S(2)}, u32[]{:S(2)}) async-start(bf16[16,2,2,800]{3,2,0,1:T(2,128)(2,1)} %copy.54), calls=%async_computation.3 | async-start | bytes 229376 | tf_op jit(solution)/shard_map/all_to_all | solution.py:63
  49.0 2.4 %all-to-all-done.3 = bf16[16,2,2,800]{3,2,0,1:T(2,128)(2,1)S(1)} async-done(((bf16[16,2,2,800]{3,2,0,1:T(2,128)(2,1)}), bf16[16,2,2,800]{3,2,0,1:T(2,128)(2,1)S(1)}, u32[]{:S(2)}, u32[]{:S(2)}) %all-to-all-start.3) | async-done | bytes 102432 | tf_op jit(solution)/shard_map/all_to_all | solution.py:63
  54.3 2.4 %copy.66 = f32[256,800]{1,0:T(8,128)} copy(f32[256,800]{0,1:T(8,128)} %fusion.41) | data formatting | bytes 1638400
  58.2 1.5 %fusion.42 = f32[256,800]{0,1:T(8,128)} fusion(bf16[256,1024]{1,0:T(8,128)(2,1)S(1)} %fusion.6, bf16[1024,800]{0,1:T(8,128)(2,1)S(1)} %convolution_convert_fusion), kind=kOutput, calls=%fused_computation.81 | convolution fusion | flops 419430400 | bytes 2981888 | tf_op jit(solution)/shard_map/while/body/eval_jaxpr/dot_general | solution.py:99
  59.7 2.3 %fusion.40 = f32[1024,800]{0,1:T(8,128)} fusion(bf16[256,1024]{1,0:T(8,128)(2,1)S(1)} %fusion.6, bf16[256,400]{0,1:T(8,128)(2,1)S(1)} %get-tuple-element.32, bf16[256,400]{0,1:T(8,128)(2,1)S(1)} %get-tuple-element.23), kind=kOutput, calls=%fused_computation.79 | convolution fusion | flops 420249600 | bytes 4210688 | tf_op jit(solution)/shard_map/while/body/eval_jaxpr/dot_general | solution.py:102
  63.4 1.4 %multiply_reduce_fusion = f32[256]{0:T(256)S(1)} fusion(f32[256,800]{1,0:T(8,128)} %copy.66, bf16[256,800]{1,0:T(8,128)(2,1)S(1)} %gather_fusion.3), kind=kLoop, calls=%fused_computation.23 | loop fusion | flops 614144 | bytes 1229824 | tf_op jit(solution)/shard_map/td,td->t/dot_general | solution.py:83
  68.5 1.7 %convert_element_type.115 = bf16[16,2,2,800]{3,2,1,0:T(2,128)(2,1)} reshape(bf16[64,800]{1,0:T(8,128)(2,1)} %fusion.10) | data formatting | bytes 204800 | tf_op jit(solution)/shard_map/convert_element_type | solution.py:134
  70.1 4.1 %all-to-all-start.4 = ((bf16[16,2,2,800]{3,2,1,0:T(2,128)(2,1)}), bf16[16,2,2,800]{3,2,1,0:T(2,128)(2,1)}, u32[]{:S(2)}, u32[]{:S(2)}) async-start(bf16[16,2,2,800]{3,2,1,0:T(2,128)(2,1)} %convert_element_type.115), calls=%async_computation.4 | async-start | bytes 229376 | tf_op jit(solution)/shard_map/all_to_all | solution.py:133
  74.4 1.7 %convolution_add_fusion.1 = f32[256,800]{0,1:T(8,128)S(1)} fusion(f32[256,800]{0,1:T(8,128)} %fusion.15, f32[256]{0:T(256)S(1)} %divide_negate_fusion, s32[256]{0:T(256)S(1)} %copy-done.10, bf16[256,400]{0,1:T(8,128)(2,1)} %copy-done.3, bf16[256,400]{0,1:T(8,128)(2,1)} %copy-done.2), kind=kOutput, calls=%fused_computation.14 | convolution fusion | flops 106971136 | bytes 2050048 | tf_op jit(solution)/shard_map/dot_general | solution.py:35
  78.2 1.5 %fusion.19 = f32[256,800]{0,1:T(8,128)S(1)} fusion(f32[256,400]{0,1:T(8,128)} %get-tuple-element.33, f32[256,400]{0,1:T(8,128)} %get-tuple-element.34, s32[256]{0:T(256)S(1)} %copy-done.9), kind=kOutput, calls=%fused_computation.39 | convolution fusion | flops 105742336 | bytes 1639424 | tf_op jit(solution)/shard_map/dot_general | solution.py:35
  80.0 2.0 %all-to-all-done.4 = bf16[16,2,2,800]{3,2,1,0:T(2,128)(2,1)} async-done(((bf16[16,2,2,800]{3,2,1,0:T(2,128)(2,1)}), bf16[16,2,2,800]{3,2,1,0:T(2,128)(2,1)}, u32[]{:S(2)}, u32[]{:S(2)}) %all-to-all-start.4) | async-done | bytes 102432 | tf_op jit(solution)/shard_map/all_to_all | solution.py:133
  82.0 1.6 %copy.61 = bf16[16,2,2,800]{3,2,0,1:T(2,128)(2,1)} copy(bf16[16,2,2,800]{3,2,1,0:T(2,128)(2,1)} %all-to-all-done.4) | data formatting | bytes 204800 | tf_op jit(solution)/shard_map/all_to_all | solution.py:133
  83.6 3.4 %all-to-all-start.5 = ((bf16[16,2,2,800]{3,2,0,1:T(2,128)(2,1)}), bf16[16,2,2,800]{3,2,0,1:T(2,128)(2,1)S(1)}, u32[]{:S(2)}, u32[]{:S(2)}) async-start(bf16[16,2,2,800]{3,2,0,1:T(2,128)(2,1)} %copy.61), calls=%async_computation.5 | async-start | bytes 229376 | tf_op jit(solution)/shard_map/all_to_all | solution.py:132
  87.0 13.4 %all-gather = bf16[512,800]{0,1:T(8,128)(2,1)S(1)} all-gather(bf16[256,800]{0,1:T(8,128)(2,1)S(1)} %fusion.7), channel_id=2, replica_groups=mesh['blk'=16,'rel'=2] {'rel'}, dimensions={0}, use_global_device_ids=true | all-gather | bytes 1228800 | tf_op jit(solution)/shard_map/all_gather | solution.py:128
  100.6 2.9 %reduce_sum.12 = bf16[256,800]{0,1:T(8,128)(2,1)} reduce(bf16[2,256,800]{1,0,2:T(2,128)(2,1)S(1)} %reshape.121, bf16[]{:T(256)} %constant.24.clone.1), dimensions={0}, to_apply=%region_0.1 | reduce | flops 204800 | bytes 1228802 | tf_op jit(solution)/shard_map/reduce_sum | solution.py:128
  104.5 2.6 %all-reduce.2.cloned.1.call-done = bf16[256,800]{0,1:T(8,128)(2,1)} async-done(((bf16[256,800]{0,1:T(8,128)(2,1)}), bf16[256,800]{0,1:T(8,128)(2,1)}) %all-reduce.2.cloned.1.call-update) | async-done | bytes 409616 | tf_op jit(solution)/shard_map/psum | solution.py:129
  107.1 1.8 %copy.68 = bf16[256,800]{0,1:T(8,128)(2,1)} copy(bf16[256,800]{0,1:T(8,128)(2,1)} %all-reduce.2.cloned.1.call-done) | data formatting | bytes 819200
  (76 shorter events, 21.8 us)
Async XLA Ops:
  7.2 23.2 %copy-start = (bf16[32,800]{1,0:T(8,128)(2,1)S(1)}, bf16[32,800]{1,0:T(8,128)(2,1)}, u32[]{:S(2)}) copy-start(bf16[32,800]{1,0:T(8,128)(2,1)} %param.11) | copy-start | bytes 153604
  7.2 28.2 %copy-start.10 = (s32[256]{0:T(256)S(1)}, s32[256]{0:T(256)}, u32[]{:S(2)}) copy-start(s32[256]{0:T(256)} %param.13) | copy-start | bytes 3076
  7.2 39.9 %copy-start.7 = (bf16[256,800]{0,1:T(8,128)(2,1)S(1)}, bf16[256,800]{0,1:T(8,128)(2,1)}, u32[]{:S(2)}) copy-start(bf16[256,800]{0,1:T(8,128)(2,1)} %param.9) | copy-start | bytes 1228804
  8.6 13.9 %all-to-all-start = ((s32[16,2,2]{2,1,0:T(2,128)}), s32[16,2,2]{2,1,0:T(2,128)S(1)}, u32[]{:S(2)}, u32[]{:S(2)}) async-start(s32[16,2,2]{2,1,0:T(2,128)} %copy.51), calls=%async_computation | async-start | bytes 32768 | tf_op jit(solution)/shard_map/all_to_all | solution.py:56
  17.3 39.4 %collective-permute-start = (bf16[256,800]{1,0:T(8,128)(2,1)S(1)}, bf16[256,800]{1,0:T(8,128)(2,1)S(1)}, u32[]{:S(2)}, u32[]{:S(2)}) collective-permute-start(bf16[256,800]{1,0:T(8,128)(2,1)S(1)} %copy.57), channel_id=1, source_target_pairs={{0,2},{2,4},{4,6},{6,8},{8,10},{10,12},{12,14},{14,16},{16,18},{18... | collective-permute-start | bytes 1228808 | tf_op jit(solution)/shard_map/ppermute | solution.py:9
  23.2 7.0 %all-to-all-start.1 = ((s32[16,2,2]{0,2,1:T(2,128)}), s32[16,2,2]{0,2,1:T(2,128)S(1)}, u32[]{:S(2)}, u32[]{:S(2)}) async-start(s32[16,2,2]{0,2,1:T(2,128)} %copy.52), calls=%async_computation.1 | async-start | bytes 4096 | tf_op jit(solution)/shard_map/all_to_all | solution.py:55
  31.8 11.2 %all-to-all-start.2 = ((bf16[16,2,2,800]{3,2,1,0:T(2,128)(2,1)}), bf16[16,2,2,800]{3,2,1,0:T(2,128)(2,1)S(1)}, u32[]{:S(2)}, u32[]{:S(2)}) async-start(bf16[16,2,2,800]{3,2,1,0:T(2,128)(2,1)} %reshape.86), calls=%async_computation.2 | async-start | bytes 229376 | tf_op jit(solution)/shard_map/all_to_all | solution.py:64
  43.7 7.7 %all-to-all-start.3 = ((bf16[16,2,2,800]{3,2,0,1:T(2,128)(2,1)}), bf16[16,2,2,800]{3,2,0,1:T(2,128)(2,1)S(1)}, u32[]{:S(2)}, u32[]{:S(2)}) async-start(bf16[16,2,2,800]{3,2,0,1:T(2,128)(2,1)} %copy.54), calls=%async_computation.3 | async-start | bytes 229376 | tf_op jit(solution)/shard_map/all_to_all | solution.py:63
  53.2 11.6 %copy-start.2 = (bf16[256,400]{0,1:T(8,128)(2,1)}, bf16[256,400]{0,1:T(8,128)(2,1)S(1)}, u32[]{:S(2)}) copy-start(bf16[256,400]{0,1:T(8,128)(2,1)S(1)} %get-tuple-element.23) | copy-start | bytes 614404
  53.2 11.6 %copy-start.3 = (bf16[256,400]{0,1:T(8,128)(2,1)}, bf16[256,400]{0,1:T(8,128)(2,1)S(1)}, u32[]{:S(2)}) copy-start(bf16[256,400]{0,1:T(8,128)(2,1)S(1)} %get-tuple-element.32) | copy-start | bytes 614404
  53.2 3.4 %copy-start.8 = (s32[1,1024]{1,0:T(1,128)S(1)}, s32[1,1024]{1,0:T(1,128)}, u32[]{:S(2)}) copy-start(s32[1,1024]{1,0:T(1,128)} %param.15) | copy-start | bytes 12292
  63.4 2.7 %copy-start.6 = (f32[256,800]{0,1:T(8,128)S(1)}, f32[256,800]{0,1:T(8,128)}, u32[]{:S(2)}) copy-start(f32[256,800]{0,1:T(8,128)} %fusion.42) | copy-start | bytes 2457604
  66.2 1.1 copy-start.11
  67.5 8.5 %copy-start.1 = (f32[1024,800]{0,1:T(8,128)S(1)}, f32[1024,800]{0,1:T(8,128)}, u32[]{:S(2)}) copy-start(f32[1024,800]{0,1:T(8,128)} %fusion.40) | copy-start | bytes 9830404
  70.1 11.8 %all-to-all-start.4 = ((bf16[16,2,2,800]{3,2,1,0:T(2,128)(2,1)}), bf16[16,2,2,800]{3,2,1,0:T(2,128)(2,1)}, u32[]{:S(2)}, u32[]{:S(2)}) async-start(bf16[16,2,2,800]{3,2,1,0:T(2,128)(2,1)} %convert_element_type.115), calls=%async_computation.4 | async-start | bytes 229376 | tf_op jit(solution)/shard_map/all_to_all | solution.py:133
  74.3 32.8 %all-reduce.2.cloned.1.call-start = ((), (), s32[]{:S(2)}) async-start(), calls=%async_computation.6 | async-start | bytes 819200 | tf_op jit(solution)/shard_map/psum | solution.py:129
  76.7 1.5 %copy-start.9 = (s32[256]{0:T(256)S(1)}, s32[256]{0:T(256)}, u32[]{:S(2)}) copy-start(s32[256]{0:T(256)} %param.12) | copy-start | bytes 3076
  78.1 1.5 %copy-start.4 = (f32[256,400]{0,1:T(8,128)S(1)}, f32[256,400]{0,1:T(8,128)}, u32[]{:S(2)}) copy-start(f32[256,400]{0,1:T(8,128)} %get-tuple-element.33) | copy-start | bytes 1228804
  78.1 1.5 %copy-start.5 = (f32[256,400]{0,1:T(8,128)S(1)}, f32[256,400]{0,1:T(8,128)}, u32[]{:S(2)}) copy-start(f32[256,400]{0,1:T(8,128)} %get-tuple-element.34) | copy-start | bytes 1228804
  83.6 19.9 %all-to-all-start.5 = ((bf16[16,2,2,800]{3,2,0,1:T(2,128)(2,1)}), bf16[16,2,2,800]{3,2,0,1:T(2,128)(2,1)S(1)}, u32[]{:S(2)}, u32[]{:S(2)}) async-start(bf16[16,2,2,800]{3,2,0,1:T(2,128)(2,1)} %copy.61), calls=%async_computation.5 | async-start | bytes 229376 | tf_op jit(solution)/shard_map/all_to_all | solution.py:132
Sparse Core Ops, SparseCore 0:
  78.3 28.7 all-reduce.1
